TPU v7x, 128 devices: a whole 4x4x4 slice. The times are simulated.
128 devices in a mesh: pix: 8 (over y_hi, z), tm: 16 (over x, y_lo, core).
Axes of the slice: x: 4, y: 4 (y_hi: 2, y_lo: 2; y = y_hi * 2 + y_lo), z: 4, core: 2. Of those that a mesh axis runs over, the one named last changes fastest.
Arguments:
- frames: float32 [16, 192, 12288], P('tm', 'pix'), may hold values from 0.05 to 5
- pixel_order: int32 [12288], replicated, may hold values from 0 to 12287, each once
- cycle_sizes: int32 [64], replicated, may hold values from 1 to 384, 12288 in all
- kernel: float32 [5], replicated, may hold values from 0.1 to 1
Outputs:
- correlation: float32 [64, 3072, 3072], P('pix', 'tm')
Inputs may be any that keep to these rules, and one draw needn't show every extreme that they name: `cycle_sizes`: every cycle has one or more pixels, the sizes sum to 12288, and one cycle has exactly 384.
All inputs are finite; a program needn't handle non-finite values.
Results may differ from a plain program's by a relative error of at most 0.00005.
Values sent between devices are 32-bit elements; how exact they have to be, the bound alone decides.
No kernel may reach another device: no remote copies, remote signals or barrier semaphores. Data moves between devices by JAX's collectives and lax.ppermute only.
A program may use at most 256 MiB of HBM per device.

v0:
```python
import jax
import jax.numpy as jnp
from jax import lax
from jax.sharding import PartitionSpec as P

REACH = 2


def with_halo(block, sides, width):
    for axis, dim in sides:
        count = lax.axis_size(axis)
        forward = [(i, i + 1) for i in range(count - 1)]
        backward = [(target, source) for source, target in forward]
        low = lax.ppermute(
            lax.slice_in_dim(block, block.shape[dim] - width, None, axis=dim), axis, forward
        )
        high = lax.ppermute(lax.slice_in_dim(block, 0, width, axis=dim), axis, backward)
        block = jnp.concatenate([low, block, high], axis=dim)
    return block


def correlate(left, left_total, right, scale):
    product = jnp.einsum(
        "rct,rcs->rts",
        left,
        right,
        precision=lax.Precision.HIGHEST,
        preferred_element_type=jnp.float32,
    )
    right_total = jnp.sum(right, axis=1)
    return product * scale[:, None, None] / (left_total[:, :, None] * right_total[:, None, :])


def per_device(frames, pixel_order, cycle_sizes, kernel):
    block = frames[0]
    cycles = cycle_sizes.shape[0]
    pixels = block.shape[1]
    cap = 2 * pixels // cycles
    starts = jnp.cumsum(cycle_sizes) - cycle_sizes
    slots = jnp.arange(cap, dtype=jnp.int32)
    where_idx = jnp.minimum(starts[:, None] + slots[None, :], pixels - 1)
    valid = slots[None, :] < cycle_sizes[:, None]
    columns = pixel_order[where_idx]
    flat = jnp.transpose(block)
    picked = jnp.where(valid[:, :, None], flat[columns], 0.0)
    local = lax.all_to_all(picked, "pix", split_axis=0, concat_axis=2, tiled=True)
    owned = local.shape[0]
    tblk = local.shape[2]
    scale = lax.dynamic_slice_in_dim(cycle_sizes, lax.axis_index("pix") * owned, owned).astype(
        jnp.float32
    )
    own_total = jnp.sum(local, axis=1)
    normed = correlate(local, own_total, lax.all_gather(local, "tm", axis=2, tiled=True), scale)
    count = normed.shape[2]
    padded = jnp.pad(normed, ((0, 0), (0, 0), (REACH, REACH)))
    across = kernel[0] * padded[:, :, 0:count]
    for shift_step in range(1, 2 * REACH + 1):
        across = across + kernel[shift_step] * padded[:, :, shift_step : shift_step + count]
    rimmed = with_halo(across, (("tm", 1),), REACH)
    result = kernel[0] * rimmed[:, 0:tblk]
    for shift_step in range(1, 2 * REACH + 1):
        result = result + kernel[shift_step] * rimmed[:, shift_step : shift_step + tblk]
    return result


def solution(mesh):
    placed = (P("tm", "pix", None), P(), P(), P())
    return jax.shard_map(
        per_device, mesh=mesh, in_specs=placed, out_specs=P("pix", "tm", None), check_vma=False
    )
```

profile of v0, /device:TPU:1, one launch (start us, length us, event | category | flops | bytes accessed | tf_op | source)
XLA Modules:
  0.0 637.4 jit_solution(14035396235880347617)
XLA Ops:
  6.5 0.0 copy-start
  6.5 0.0 all-gather.2.cloned.1.call-start
  6.5 4.9 copy.15
  11.4 0.7 iota_compare_fusion
  12.2 0.7 copy.16
  12.9 0.1 reduce-window.9
  13.0 0.1 reduce.1
  13.1 0.7 sub.3
  13.8 0.1 compare_select_fusion.1
  13.9 0.0 copy-done
  13.9 135.5 %gather_fusion = s32[24576]{0:T(1024)S(1)} fusion(s32[12288]{0:T(1024)S(1)} %copy-done, s32[24576]{0:T(1024)S(1)} %broadcast_clamp_fusion), kind=kCustom, calls=%fused_computation | custom fusion | bytes 294912 | tf_op jit(solution)/shard_map/gather | solution.py:43
  149.6 84.8 %gather_fusion.1 = f32[24576,24]{1,0:T(8,128)} fusion(f32[12288,24]{1,0:T(8,128)} %bitcast.20, s32[24576]{0:T(1024)S(1)} %broadcast_clamp_fusion.1), kind=kCustom, calls=%fused_computation.1 | custom fusion | bytes 4816896 | tf_op jit(solution)/shard_map/gather | solution.py:45
  234.4 0.0 copy-start.4
  234.4 0.0 copy-start.3
  234.4 7.7 %copy.17 = f32[64,384,24]{1,2,0:T(8,128)S(1)} copy(f32[64,384,24]{2,1,0:T(8,128)} %bitcast.21) | data formatting | bytes 4718592 | tf_op jit(solution)/shard_map/gather | solution.py:45
  242.1 0.3 broadcast_select_fusion
  242.4 38.0 %all_to_all.18 = f32[64,384,24]{1,2,0:T(8,128)S(1)} all-to-all(f32[64,384,24]{1,2,0:T(8,128)S(1)} %broadcast_select_fusion), channel_id=1, replica_groups=mesh['pix'=8,'tm'=16] {'pix'}, dimensions={0} | all-to-all | bytes 4718592 | tf_op jit(solution)/shard_map/all_to_all | solution.py:46
  280.4 1.6 copy.18
  282.0 0.0 all-gather.2.cloned.1.call-update
  282.0 0.0 copy-done.4
  282.0 0.1 dynamic-slice_convert_fusion
  282.1 0.0 copy-done.3
  282.1 0.7 fusion.12
  282.7 0.3 reduce_sum.18
  283.0 0.1 mul.80
  283.1 0.0 copy-start.2
  283.1 188.8 %all-gather.2.cloned.1.call-done = f32[8,384,3072]{1,2,0:T(8,128)} async-done(((f32[8,384,192]{1,2,0:T(8,128)}), f32[8,384,3072]{1,2,0:T(8,128)}) %all-gather.2.cloned.1.call-update) | async-done | bytes 37748752 | tf_op jit(solution)/shard_map/all_gather | solution.py:53
  471.9 17.3 %reduce_sum.19 = f32[8,3072]{1,0:T(8,128)S(1)} reduce(f32[8,384,3072]{1,2,0:T(8,128)} %all-gather.2.cloned.1.call-done, f32[]{:T(128)} %constant.6.clone.1), dimensions={1}, to_apply=%region_2.3 | reduce | flops 9412608 | bytes 37847044 | tf_op jit(solution)/shard_map/reduce_sum | solution.py:30
  489.2 0.0 copy-done.2
  489.2 47.2 %multiply_divide_fusion = f32[8,192,3072]{2,1,0:T(8,128)} fusion(f32[8,3072]{1,0:T(8,128)S(1)} %reduce_sum.19, f32[8,192]{1,0:T(8,128)S(1)} %mul.80, f32[8]{0:T(128)S(1)} %dynamic-slice_convert_fusion, f32[8,384,192]{1,2,0:T(8,128)S(1)} %bitcast.25, f32[8,384,3072]{1,2,0:T(8,128)} %all-gather.2.cloned.1.call-done), kind=kOutput, calls=%fused_computation.21 | convolution fusion | flops 21757427712 | bytes 59086880 | tf_op jit(solution)/shard_map/rct,rcs->rts/dot_general | solution.py:23
  536.4 41.1 %multiply_add_fusion = f32[8,192,3072]{2,1,0:T(8,128)} fusion(f32[8,192,3072]{2,1,0:T(8,128)} %multiply_divide_fusion, f32[]{:T(128)} %bitcast.12, f32[]{:T(128)} %bitcast.11, f32[]{:T(128)} %bitcast.10, f32[]{:T(128)} %bitcast.9, f32[]{:T(128)} %bitcast), kind=kLoop, calls=%fused_computation.18 | loop fusion | flops 42467328 | bytes 37748756 | tf_op jit(solution)/shard_map/add | solution.py:58
  577.5 1.5 fusion.11
  579.0 3.2 collective-permute-start
  582.2 0.0 copy-start.1
  582.3 2.1 collective-permute-start.1
  584.3 0.5 collective-permute-done
  584.8 4.5 collective-permute-done.1
  589.4 41.1 %fusion.3 = f32[8,192,3072]{2,1,0:T(8,128)} fusion(f32[8,192,3072]{2,1,0:T(8,128)} %multiply_add_fusion, f32[8,2,3072]{2,1,0:T(2,128)S(1)} %collective-permute-done.1, f32[8,2,3072]{2,1,0:T(2,128)S(1)} %collective-permute-done, f32[]{:T(128)} %bitcast.12, f32[]{:T(128)} %bitcast.11, f32[]{:T(128)} %bitcast.10, f32[]{:T(128)} %bitcast.9, f32[]{:T(128)} %bitcast), kind=kLoop, calls=%fused_computation.9 | loop fusion | flops 61341696 | bytes 38141972 | tf_op jit(solution)/shard_map/add | solution.py:62
  630.5 0.0 copy-done.1
  (7 shorter events, 0.1 us)
Async XLA Ops:
  6.5 7.4 %copy-start = (s32[12288]{0:T(1024)S(1)}, s32[12288]{0:T(1024)}, u32[]{:S(2)}) copy-start(s32[12288]{0:T(1024)} %param.5) | copy-start | bytes 147460
  6.5 465.3 %all-gather.2.cloned.1.call-start = ((), (), s32[]{:S(2)}) async-start(), calls=%async_computation.1 | async-start | bytes 40108032 | tf_op jit(solution)/shard_map/all_gather | solution.py:53
  234.4 47.5 %copy-start.4 = (s32[64]{0:T(128)S(1)}, s32[64]{0:T(128)}, u32[]{:S(2)}) copy-start(s32[64]{0:T(128)} %param.6) | copy-start | bytes 772
  234.4 47.6 %copy-start.3 = (f32[5]{0:T(128)S(1)}, f32[5]{0:T(128)}, u32[]{:S(2)}) copy-start(f32[5]{0:T(128)} %param.7) | copy-start | bytes 64
  283.1 206.1 %copy-start.2 = (f32[8,384,8,24]{1,3,2,0:T(8,128)S(1)}, f32[8,384,8,24]{1,3,2,0:T(8,128)}, u32[]{:S(2)}) copy-start(f32[8,384,8,24]{1,3,2,0:T(8,128)} %copy.18) | copy-start | bytes 7077892
  579.0 5.8 collective-permute-start
  582.2 48.3 %copy-start.1 = (s32[12288]{0:T(1024)S(1)}, s32[12288]{0:T(1024)}, u32[]{:S(2)}) copy-start(s32[12288]{0:T(1024)} %param.5) | copy-start | bytes 147460
  582.3 7.1 %collective-permute-start.1 = (f32[8,2,3072]{2,1,0:T(2,128)S(1)}, f32[8,2,3072]{2,1,0:T(2,128)S(1)}, u32[]{:S(2)}, u32[]{:S(2)}) collective-permute-start(f32[8,2,3072]{2,1,0:T(2,128)S(1)} %get-tuple-element.6), channel_id=1, source_target_pairs={{1,0},{2,1},{3,2},{4,3},{5,4},{6,5},{7,6},{8,7},{9,8},{10,9},{11,1... | collective-permute-start | bytes 589832 | tf_op jit(solution)/shard_map/ppermute | solution.py:17
Sparse Core Ops, SparseCore 0:
  282.1 189.7 all-gather.1
where the time goes:
time: 638 us; the launch traced here: 637 us
  local copies, waits for them, and re-layouts  238 us (37%)
  waiting for transfers between devices  194 us (30%)
  other arithmetic  102 us (16%)
  matrix products  47.2 us (7%)
  blocking collectives  38 us (6%)
  between operations  13.6 us (2%)
    all_gather x1, waiting for transfers between devices, per_device(): lax.all_gather(local, 'tm', axis=2, tiled=True)  189 us
    gather x2, local copies, waits for them, and re-layouts, per_device(): columns = pixel_order[where_idx]  136 us
    gather x2, local copies, waits for them, and re-layouts, per_device(): picked = jnp.where(valid[:, :, None], flat[columns], 0.0)  92.5 us
    dot_general x1, matrix products, correlate(): jnp.einsum('rct,rcs->rts', left, right, precision=lax.Precision.HIGHEST,...  47.2 us
    add x1, other arithmetic, per_device(): result + kernel[shift_step] * rimmed[:, shift_step:shift_step + tblk]  41.1 us
    add x1, other arithmetic, per_device(): across + kernel[shift_step] * padded[:, :, shift_step:shift_step + count]  41.1 us
    all_to_all x1, blocking collectives, per_device(): lax.all_to_all(picked, 'pix', split_axis=0, concat_axis=2, tiled=True)  38 us
    reduce_sum x1, other arithmetic, correlate(): right_total = jnp.sum(right, axis=1)  17.3 us
  transfers between devices with their start and end apart: 3, of which 3 were waited for; matrix products, arithmetic and copies ran while one was open for 0% of the time, Pallas kernels for 0%

commit v1 on v0

--- a/solution.py
+++ b/solution.py
@@ -43,7 +43,10 @@
     columns = pixel_order[where_idx]
     flat = jnp.transpose(block)
     picked = jnp.where(valid[:, :, None], flat[columns], 0.0)
-    local = lax.all_to_all(picked, "pix", split_axis=0, concat_axis=2, tiled=True)
+    local = jnp.concatenate(
+        lax.all_to_all(jnp.stack(jnp.split(picked, lax.axis_size("pix"), axis=0)), "pix", 0, 0),
+        axis=2,
+    )
     owned = local.shape[0]
     tblk = local.shape[2]
     scale = lax.dynamic_slice_in_dim(cycle_sizes, lax.axis_index("pix") * owned, owned).astype(

time: 638 us -> 638 us (level)
  no operation moved by 1% of the time
where the time goes in v1:
time: 638 us
  local copies, waits for them, and re-layouts  238 us (37%)
  waiting for transfers between devices  194 us (30%)
  other arithmetic  102 us (16%)
  matrix products  47.2 us (7%)
  blocking collectives  38 us (6%)
  between operations  13.6 us (2%)
    all_gather x1, waiting for transfers between devices, per_device(): lax.all_gather(local, 'tm', axis=2, tiled=True)  189 us
    gather x2, local copies, waits for them, and re-layouts, per_device(): columns = pixel_order[where_idx]  136 us
    gather x2, local copies, waits for them, and re-layouts, per_device(): picked = jnp.where(valid[:, :, None], flat[columns], 0.0)  92.5 us
    dot_general x1, matrix products, correlate(): jnp.einsum('rct,rcs->rts', left, right, precision=lax.Precision.HIGHEST,...  47.2 us
    add x1, other arithmetic, per_device(): result + kernel[shift_step] * rimmed[:, shift_step:shift_step + tblk]  41.1 us
    add x1, other arithmetic, per_device(): across + kernel[shift_step] * padded[:, :, shift_step:shift_step + count]  41.1 us
    all_to_all x1, blocking collectives, per_device(): lax.all_to_all(jnp.stack(jnp.split(picked, lax.axis_size('pix'), axis=0))...  38 us
    reduce_sum x1, other arithmetic, correlate(): right_total = jnp.sum(right, axis=1)  17.3 us
  transfers between devices with their start and end apart: 3, of which 3 were waited for; matrix products, arithmetic and copies ran while one was open for 0% of the time, Pallas kernels for 0%

profile of v1, /device:TPU:1, one launch (start us, length us, event | category | flops | bytes accessed | tf_op | source)
XLA Modules:
  0.0 637.6 jit_solution(10149181997880742596)
XLA Ops:
  6.5 0.0 copy-start
  6.5 0.0 all-gather.2.cloned.1.call-start
  6.5 4.9 copy.33
  11.4 0.7 iota_compare_fusion
  12.2 0.7 copy.34
  12.9 0.1 reduce-window.9
  13.0 0.1 reduce.1
  13.1 0.7 sub.3
  13.8 0.1 compare_select_fusion.1
  13.9 0.0 copy-done
  13.9 135.5 %gather_fusion = s32[24576]{0:T(1024)S(1)} fusion(s32[12288]{0:T(1024)S(1)} %copy-done, s32[24576]{0:T(1024)S(1)} %broadcast_clamp_fusion), kind=kCustom, calls=%fused_computation | custom fusion | bytes 294912 | tf_op jit(solution)/shard_map/gather | solution.py:43
  149.6 84.8 %gather_fusion.1 = f32[24576,24]{1,0:T(8,128)} fusion(f32[12288,24]{1,0:T(8,128)} %bitcast.51, s32[24576]{0:T(1024)S(1)} %broadcast_clamp_fusion.1), kind=kCustom, calls=%fused_computation.1 | custom fusion | bytes 4816896 | tf_op jit(solution)/shard_map/gather | solution.py:45
  234.4 0.0 copy-start.4
  234.4 0.0 copy-start.3
  234.4 7.7 %copy.35 = f32[64,384,24]{1,2,0:T(8,128)S(1)} copy(f32[64,384,24]{2,1,0:T(8,128)} %bitcast.52) | data formatting | bytes 4718592 | tf_op jit(solution)/shard_map/gather | solution.py:45
  242.1 0.3 broadcast_select_fusion
  242.6 38.0 %all_to_all.5 = f32[8,8,384,24]{2,3,1,0:T(8,128)S(1)} all-to-all(f32[8,8,384,24]{2,3,1,0:T(8,128)S(1)} %fusion.11), channel_id=1, replica_groups=mesh['pix'=8,'tm'=16] {'pix'}, dimensions={0} | all-to-all | bytes 4718592 | tf_op jit(solution)/shard_map/all_to_all | solution.py:47
  280.6 1.6 copy.36
  282.2 0.0 all-gather.2.cloned.1.call-update
  282.2 0.0 copy-done.4
  282.2 0.1 dynamic-slice_convert_fusion
  282.3 0.0 copy-done.3
  282.3 0.7 fusion.20
  283.0 0.3 bitcast_reduce_fusion
  283.3 0.1 mul.80
  283.3 0.0 copy-start.2
  283.3 188.8 %all-gather.2.cloned.1.call-done = f32[8,384,3072]{1,2,0:T(8,128)} async-done(((f32[8,384,192]{1,2,0:T(8,128)}), f32[8,384,3072]{1,2,0:T(8,128)}) %all-gather.2.cloned.1.call-update) | async-done | bytes 37748752 | tf_op jit(solution)/shard_map/all_gather | solution.py:56
  472.1 17.3 %reduce_sum.19 = f32[8,3072]{1,0:T(8,128)S(1)} reduce(f32[8,384,3072]{1,2,0:T(8,128)} %all-gather.2.cloned.1.call-done, f32[]{:T(128)} %constant.6.clone.1), dimensions={1}, to_apply=%region_2.3 | reduce | flops 9412608 | bytes 37847044 | tf_op jit(solution)/shard_map/reduce_sum | solution.py:30
  489.4 0.0 copy-done.2
  489.4 47.2 %multiply_divide_fusion = f32[8,192,3072]{2,1,0:T(8,128)} fusion(f32[8,3072]{1,0:T(8,128)S(1)} %reduce_sum.19, f32[8,192]{1,0:T(8,128)S(1)} %mul.80, f32[8]{0:T(128)S(1)} %dynamic-slice_convert_fusion, f32[8,384,192]{1,2,0:T(8,128)S(1)} %bitcast.55, f32[8,384,3072]{1,2,0:T(8,128)} %all-gather.2.cloned.1.call-done), kind=kOutput, calls=%fused_computation.21 | convolution fusion | flops 21757427712 | bytes 59086880 | tf_op jit(solution)/shard_map/rct,rcs->rts/dot_general | solution.py:23
  536.7 41.1 %multiply_add_fusion = f32[8,192,3072]{2,1,0:T(8,128)} fusion(f32[8,192,3072]{2,1,0:T(8,128)} %multiply_divide_fusion, f32[]{:T(128)} %bitcast.18, f32[]{:T(128)} %bitcast.17, f32[]{:T(128)} %bitcast.16, f32[]{:T(128)} %bitcast.15, f32[]{:T(128)} %bitcast), kind=kLoop, calls=%fused_computation.18 | loop fusion | flops 42467328 | bytes 37748756 | tf_op jit(solution)/shard_map/add | solution.py:61
  577.7 1.5 fusion.19
  579.2 3.2 collective-permute-start
  582.5 0.0 copy-start.1
  582.5 2.1 collective-permute-start.1
  584.6 0.5 collective-permute-done
  585.1 4.5 collective-permute-done.1
  589.6 41.1 %fusion.3 = f32[8,192,3072]{2,1,0:T(8,128)} fusion(f32[8,192,3072]{2,1,0:T(8,128)} %multiply_add_fusion, f32[8,2,3072]{2,1,0:T(2,128)S(1)} %collective-permute-done.1, f32[8,2,3072]{2,1,0:T(2,128)S(1)} %collective-permute-done, f32[]{:T(128)} %bitcast.18, f32[]{:T(128)} %bitcast.17, f32[]{:T(128)} %bitcast.16, f32[]{:T(128)} %bitcast.15, f32[]{:T(128)} %bitcast), kind=kLoop, calls=%fused_computation.9 | loop fusion | flops 61341696 | bytes 38141972 | tf_op jit(solution)/shard_map/add | solution.py:65
  630.8 0.0 copy-done.1
  (15 shorter events, 0.3 us)
Async XLA Ops:
  6.5 7.4 %copy-start = (s32[12288]{0:T(1024)S(1)}, s32[12288]{0:T(1024)}, u32[]{:S(2)}) copy-start(s32[12288]{0:T(1024)} %param.5) | copy-start | bytes 147460
  6.5 465.6 %all-gather.2.cloned.1.call-start = ((), (), s32[]{:S(2)}) async-start(), calls=%async_computation.1 | async-start | bytes 40108032 | tf_op jit(solution)/shard_map/all_gather | solution.py:56
  234.4 47.8 %copy-start.4 = (s32[64]{0:T(128)S(1)}, s32[64]{0:T(128)}, u32[]{:S(2)}) copy-start(s32[64]{0:T(128)} %param.6) | copy-start | bytes 772
  234.4 47.9 %copy-start.3 = (f32[5]{0:T(128)S(1)}, f32[5]{0:T(128)}, u32[]{:S(2)}) copy-start(f32[5]{0:T(128)} %param.7) | copy-start | bytes 64
  283.3 206.1 %copy-start.2 = (f32[8,384,8,24]{1,3,2,0:T(8,128)S(1)}, f32[8,384,8,24]{1,3,2,0:T(8,128)}, u32[]{:S(2)}) copy-start(f32[8,384,8,24]{1,3,2,0:T(8,128)} %copy.36) | copy-start | bytes 7077892
  579.2 5.8 collective-permute-start
  582.5 48.3 %copy-start.1 = (s32[12288]{0:T(1024)S(1)}, s32[12288]{0:T(1024)}, u32[]{:S(2)}) copy-start(s32[12288]{0:T(1024)} %param.5) | copy-start | bytes 147460
  582.5 7.1 %collective-permute-start.1 = (f32[8,2,3072]{2,1,0:T(2,128)S(1)}, f32[8,2,3072]{2,1,0:T(2,128)S(1)}, u32[]{:S(2)}, u32[]{:S(2)}) collective-permute-start(f32[8,2,3072]{2,1,0:T(2,128)S(1)} %get-tuple-element.6), channel_id=1, source_target_pairs={{1,0},{2,1},{3,2},{4,3},{5,4},{6,5},{7,6},{8,7},{9,8},{10,9},{11,1... | collective-permute-start | bytes 589832 | tf_op jit(solution)/shard_map/ppermute | solution.py:17
Sparse Core Ops, SparseCore 0:
  282.3 189.7 all-gather.1
